TPU v7x, 256 devices: a whole 4x4x8 slice. The times are simulated.
256 devices in a mesh: blk: 64 (over z_hi, x, y, core), path: 4 (over z_lo).
Axes of the slice: x: 4, y: 4, z: 8 (z_hi: 2, z_lo: 4; z = z_hi * 4 + z_lo), core: 2. Of those that a mesh axis runs over, the one named last changes fastest.
Arguments:
- records: bfloat16 [65536, 512], P('blk'), may hold values from -87.98545 to 87.98545
- coefficients: float32 [65536, 64], P('blk', 'path'), may hold values from -6 to 6
- velocity: float32 [65536, 64], P('blk', 'path'), may hold values from -3 to 3
- targets: float32 [65536, 64], P('blk', 'path'), may hold values from -6 to 6
- block_local: int32 [3, 1536], P(None, 'blk'), may hold values from 0 to 1023
- block_count: int32 [3, 64], replicated, may hold values from 1 to 24, 1024 in all within a row
- candidates: bfloat16 [32768, 512], P('blk'), may hold values from -87.98545 to 87.98545
- frequencies: bfloat16 [512, 1024], replicated, may hold values from -0.25 to 0.25
- phases: float32 [1024], replicated, may hold values from -3.140625 to 3.140625
- prior_weight: float32 [1024, 64], P(None, 'path'), may hold values from -6 to 6
Outputs:
- coefficients_out: float32 [65536, 64], P('blk', 'path')
- velocity_out: float32 [65536, 64], P('blk', 'path')
- scores: float32 [32768, 64], P('blk', 'path')
- path_rms: float32 [32768], P('blk')
Inputs may be any that keep to these rules, and one draw needn't show every extreme that they name: `block_count`: each row sums to 1024, and its largest entry is exactly 24. `block_local`: index within the owner's records; a slot at or beyond the owner's count in that step is not used. Used entries of one owner may repeat.
All inputs are finite; a program needn't handle non-finite values.
Results may differ from a plain program's by a relative error of at most 0.0014.
Values may be sent and summed in bfloat16 or wider, within the bound.
No kernel may reach another device: no remote copies, remote signals or barrier semaphores. Data moves between devices by JAX's collectives and lax.ppermute only.
A program may use at most 128 MiB of HBM per device.

v0:
```python
import math

import jax
import jax.numpy as jnp
from jax import lax
from jax.sharding import PartitionSpec as P

NOISE = 0.5
MOMENTUM = 0.9
RATE = 0.3
EPSILON = 1e-06
SIGNAL = 9.0


def passed_along(shard, axis, by):
    length = lax.axis_size(axis)
    return lax.ppermute(shard, axis, [(i, (i + by) % length) for i in range(length)])


def square_norms(row_block):
    widened = row_block.astype(jnp.float32)
    return jnp.sum(widened * widened, axis=1)


def kernel_apply(left_rows, left_norms, right_rows, right_norms, weights):
    dot_values = lax.dot_general(
        left_rows, right_rows, (((1,), (1,)), ((), ())), preferred_element_type=jnp.float32
    )
    distance = left_norms[:, None] + right_norms[None, :] - 2.0 * dot_values
    kernel_tile = SIGNAL * jnp.exp(-distance / left_rows.shape[1])
    return jnp.dot(kernel_tile, weights, precision=lax.Precision.HIGHEST)


def prior_values(cand_rows, frequencies, phases, prior_weight):
    angles = (
        jnp.dot(cand_rows, frequencies, preferred_element_type=jnp.float32) * math.sqrt(2.0)
        + phases[None, :]
    )
    features = math.sqrt(2.0 * SIGNAL / frequencies.shape[1]) * jnp.cos(angles)
    return jnp.dot(features, prior_weight, precision=lax.Precision.HIGHEST)


def shards(
    records,
    coefficients,
    velocity,
    targets,
    block_local,
    block_count,
    candidates,
    frequencies,
    phases,
    prior_weight,
):
    record_total = records.shape[0] * lax.axis_size("blk")
    root_count = jnp.sqrt(jnp.float32(record_total))
    slot_count = block_local.shape[1]
    own_index = lax.axis_index("blk")
    neighbour = passed_along(candidates, "blk", 1)
    work_norms = square_norms(records)
    slot_ids = jnp.arange(slot_count, dtype=jnp.int32)
    for repeat in range(block_local.shape[0]):
        local_rows = block_local[repeat]
        own_count = lax.dynamic_index_in_dim(block_count[repeat], own_index, 0, keepdims=False)
        is_live = slot_ids < own_count
        gathered = lax.all_gather(records[local_rows], "blk", axis=0, tiled=True)
        gathered_norms = square_norms(gathered)
        work_coefs = coefficients
        whole_sum = lax.psum(
            kernel_apply(gathered, gathered_norms, records, work_norms, work_coefs), "blk"
        )
        product = lax.dynamic_slice_in_dim(whole_sum, own_index * slot_count, slot_count, 0)
        product = product / root_count
        gradient = jnp.where(
            is_live[:, None], product + NOISE * coefficients[local_rows] - targets[local_rows], 0.0
        )
        velocity = (MOMENTUM * velocity).at[local_rows].add(-RATE * gradient)
        coefficients = coefficients + velocity
    own_sum = kernel_apply(candidates, square_norms(candidates), records, work_norms, coefficients)
    next_sum = kernel_apply(neighbour, square_norms(neighbour), records, work_norms, coefficients)
    own_sum, next_sum = (own_sum, next_sum)
    first_part = prior_values(candidates, frequencies, phases, prior_weight) + own_sum / root_count
    next_term = next_sum / root_count
    passed = passed_along(first_part, "blk", 1)
    scores = passed_along(passed + next_term, "blk", 1)
    squares_local = jnp.sum(scores * scores, axis=1)
    summed = lax.psum(squares_local, "path")
    path_rms = jnp.sqrt(summed / (scores.shape[1] * lax.axis_size("path")) + EPSILON)
    return (coefficients, velocity, scores, path_rms)


def solution(mesh):
    return jax.shard_map(
        shards,
        mesh=mesh,
        in_specs=(
            P("blk", None),
            P("blk", "path"),
            P("blk", "path"),
            P("blk", "path"),
            P(None, "blk"),
            P(),
            P("blk", None),
            P(),
            P(),
            P(None, "path"),
        ),
        out_specs=(P("blk", "path"), P("blk", "path"), P("blk", "path"), P("blk")),
        check_vma=False,
    )
```

profile of v0, /device:TPU:1, one launch (start us, length us, event | category | flops | bytes accessed | tf_op | source)
XLA Modules:
  0.0 2475.2 jit_solution(10862809576927528547)
XLA Ops:
  8.2 2.6 gather_fusion
  10.8 2.6 gather_fusion.3
  13.5 2.6 gather_fusion.6
  16.1 2.8 collective-permute-start.1
  28.2 2.1 fusion.110
  32.4 64.6 %all-gather.7.cloned.1.call-done = bf16[1536,512]{1,0:T(8,128)(2,1)} async-done(((bf16[24,512]{1,0:T(8,128)(2,1)}), bf16[1536,512]{1,0:T(8,128)(2,1)}) %all-gather.7.cloned.1.call-update) | async-done | bytes 1572880 | tf_op jit(solution)/shard_map/all_gather | solution.py:66
  98.8 3.3 fusion.106
  102.2 7.4 fusion.16
  109.9 65.2 %all-gather.9.cloned.1.call-done = bf16[1536,512]{1,0:T(8,128)(2,1)} async-done(((bf16[24,512]{1,0:T(8,128)(2,1)}), bf16[1536,512]{1,0:T(8,128)(2,1)}) %all-gather.9.cloned.1.call-update) | async-done | bytes 1572880 | tf_op jit(solution)/shard_map/all_gather | solution.py:66
  175.1 5.9 fusion.107
  181.0 72.2 %all-gather.11.cloned.1.call-done = bf16[1536,512]{1,0:T(8,128)(2,1)} async-done(((bf16[24,512]{1,0:T(8,128)(2,1)}), bf16[1536,512]{1,0:T(8,128)(2,1)}) %all-gather.11.cloned.1.call-update) | async-done | bytes 1572880 | tf_op jit(solution)/shard_map/all_gather | solution.py:66
  253.2 6.0 fusion.108
  259.6 704.5 %all-reduce.4.cloned.1.call-done = f32[1536,16]{0,1:T(8,128)} async-done(((f32[1536,16]{0,1:T(8,128)}), f32[1536,16]{0,1:T(8,128)}) %all-reduce.4.cloned.1.call-update) | async-done | bytes 98320 | tf_op jit(solution)/shard_map/psum | solution.py:69
  967.6 10.3 fusion.8
  981.4 711.6 %all-reduce.6.cloned.1.call-done = f32[1536,16]{0,1:T(8,128)} async-done(((f32[1536,16]{0,1:T(8,128)}), f32[1536,16]{0,1:T(8,128)}) %all-reduce.6.cloned.1.call-update) | async-done | bytes 98320 | tf_op jit(solution)/shard_map/psum | solution.py:69
  1693.9 3.0 scatter_fusion.1
  1698.2 10.2 fusion
  1708.5 3.1 fusion.111
  1712.2 711.4 %all-reduce.8.cloned.1.call-done = f32[1536,16]{0,1:T(8,128)} async-done(((f32[1536,16]{0,1:T(8,128)}), f32[1536,16]{0,1:T(8,128)}) %all-reduce.8.cloned.1.call-update) | async-done | bytes 98320 | tf_op jit(solution)/shard_map/psum | solution.py:69
  2425.5 4.1 fusion.63
  2429.7 9.1 fusion.60
  2443.0 2.4 fusion.69
  2447.9 9.2 collective-permute-done.2
  2457.1 9.8 psum.31
  (91 shorter events, 34.4 us)
Async XLA Ops:
  7.2 23.2 copy-start
  7.2 20.8 copy-start.1
  7.2 20.6 copy-start.3
  7.2 16.2 copy-start.10
  7.2 17.4 copy-start.12
  7.2 89.8 %all-gather.7.cloned.1.call-start = ((), (), s32[]{:S(2)}) async-start(), calls=%async_computation.3 | async-start | bytes 1597440 | tf_op jit(solution)/shard_map/all_gather | solution.py:66
  10.8 164.3 %all-gather.9.cloned.1.call-start = ((), (), s32[]{:S(2)}) async-start(), calls=%async_computation.4 | async-start | bytes 1597440 | tf_op jit(solution)/shard_map/all_gather | solution.py:66
  13.4 239.8 %all-gather.11.cloned.1.call-start = ((), (), s32[]{:S(2)}) async-start(), calls=%async_computation.5 | async-start | bytes 1597440 | tf_op jit(solution)/shard_map/all_gather | solution.py:66
  16.1 948.0 %all-reduce.4.cloned.1.call-start = ((), (), s32[]{:S(2)}) async-start(), calls=%async_computation | async-start | bytes 196608 | tf_op jit(solution)/shard_map/psum | solution.py:69
  16.1 1692.3 %collective-permute-start.1 = (bf16[512,512]{1,0:T(8,128)(2,1)}, bf16[512,512]{1,0:T(8,128)(2,1)}, u32[]{:S(2)}, u32[]{:S(2)}) collective-permute-start(bf16[512,512]{1,0:T(8,128)(2,1)} %param.16), channel_id=1, source_target_pairs={{0,4},{4,8},{8,12},{12,16},{16,20},{20,24},{24,28},{28,32},{32,36}... | collective-permute-start | bytes 1572872 | tf_op jit(solution)/shard_map/ppermute | solution.py:17
  98.8 3.3 copy-start.8
  109.6 1583.4 %all-reduce.6.cloned.1.call-start = ((), (), s32[]{:S(2)}) async-start(), calls=%async_computation.1 | async-start | bytes 196608 | tf_op jit(solution)/shard_map/psum | solution.py:69
  181.0 784.0 %copy-start.4 = (f32[1024,16]{1,0:T(8,128)S(1)}, f32[1024,16]{1,0:T(8,128)}, u32[]{:S(2)}) copy-start(f32[1024,16]{1,0:T(8,128)} %copy.34) | copy-start | bytes 196612
  253.2 6.0 copy-start.7
  966.8 0.8 copy-start.5
  977.9 1445.7 %all-reduce.8.cloned.1.call-start = ((), (), s32[]{:S(2)}) async-start(), calls=%async_computation.2 | async-start | bytes 196608 | tf_op jit(solution)/shard_map/psum | solution.py:69
  2425.4 4.2 copy-start.2
  2425.4 4.2 copy-start.9
  2425.5 4.2 copy-start.11
  2429.6 13.4 copy-start.6
  2438.8 4.2 collective-permute-start
  2445.4 11.6 collective-permute-start.2
Sparse Core Ops, SparseCore 0:
  12.2 84.7 all-gather.6
  101.2 73.8 all-gather.8
  179.3 73.8 all-gather.10
  255.7 708.4 all-reduce.3
  978.0 714.9 all-reduce.5
  1708.6 714.9 all-reduce.7
where the time goes:
time: 2490 us; the launch traced here: 2480 us
  waiting for transfers between devices  2340 us (94%)
  matrix products  66.2 us (3%)
    psum x3, waiting for transfers between devices, shards(): lax.psum(kernel_apply(gathered, gathered_norms, records, work_norms, work...  2130 us
    all_gather x3, waiting for transfers between devices, shards(): gathered = lax.all_gather(records[local_rows], 'blk', axis=0, tiled=True)  202 us
  transfers between devices with their start and end apart: 9, of which 8 were waited for; matrix products, arithmetic and copies ran while one was open for 3% of the time, Pallas kernels for 0%

commit v1 on v0

--- a/solution.py
+++ b/solution.py
@@ -40,6 +40,29 @@
     return jnp.dot(features, prior_weight, precision=lax.Precision.HIGHEST)
 
 
+def gather_blocks(block, axis):
+    length = lax.axis_size(axis)
+    flat = block.reshape(1, -1)
+    spread = jnp.broadcast_to(flat, (length, flat.shape[1]))
+    got = lax.all_to_all(spread, axis, 0, 0, tiled=True)
+    return got.reshape((length,) + block.shape)
+
+
+def sum_to_owners(partial, axis):
+    length = lax.axis_size(axis)
+    flat = partial.reshape(length, -1)
+    got = lax.all_to_all(flat, axis, 0, 0, tiled=True)
+    return jnp.sum(got, axis=0).reshape(partial.shape[1:])
+
+
+def velocity_weights(steps):
+    a, b = [], []
+    for t in range(steps):
+        a.append(sum(MOMENTUM ** u for u in range(1, t + 1)))
+        b.append([sum(MOMENTUM ** (u - 1 - s) for u in range(s + 1, t + 1)) for s in range(t)])
+    return a, b
+
+
 def shards(
     records,
     coefficients,
@@ -52,37 +75,61 @@
     phases,
     prior_weight,
 ):
-    record_total = records.shape[0] * lax.axis_size("blk")
+    n_blk = lax.axis_size("blk")
+    record_total = records.shape[0] * n_blk
     root_count = jnp.sqrt(jnp.float32(record_total))
-    slot_count = block_local.shape[1]
+    steps, slot_count = block_local.shape
     own_index = lax.axis_index("blk")
     neighbour = passed_along(candidates, "blk", 1)
     work_norms = square_norms(records)
     slot_ids = jnp.arange(slot_count, dtype=jnp.int32)
-    for repeat in range(block_local.shape[0]):
+    paths = coefficients.shape[1]
+
+    own_rows = records[block_local.reshape(-1)]
+    gathered = lax.all_gather(own_rows, "blk", axis=0, tiled=False)
+    all_rows = gathered.reshape(n_blk * steps * slot_count, -1)
+    step_rows = [
+        gathered[:, t * slot_count:(t + 1) * slot_count].reshape(n_blk * slot_count, -1)
+        for t in range(steps)
+    ]
+    step_norms = [square_norms(rows) for rows in step_rows]
+
+    start_weights = jnp.concatenate([coefficients, velocity], axis=1)
+    partial = kernel_apply(all_rows, square_norms(all_rows), records, work_norms, start_weights)
+    start_sums = sum_to_owners(partial.reshape(n_blk, steps * slot_count, 2 * paths), "blk")
+    start_sums = start_sums.reshape(steps, slot_count, 2 * paths)
+
+    a_weight, b_weight = velocity_weights(steps)
+    updates = []
+    for repeat in range(steps):
         local_rows = block_local[repeat]
         own_count = lax.dynamic_index_in_dim(block_count[repeat], own_index, 0, keepdims=False)
         is_live = slot_ids < own_count
-        gathered = lax.all_gather(records[local_rows], "blk", axis=0, tiled=True)
-        gathered_norms = square_norms(gathered)
-        work_coefs = coefficients
-        whole_sum = lax.psum(
-            kernel_apply(gathered, gathered_norms, records, work_norms, work_coefs), "blk"
-        )
-        product = lax.dynamic_slice_in_dim(whole_sum, own_index * slot_count, slot_count, 0)
-        product = product / root_count
+        mine = own_rows[repeat * slot_count:(repeat + 1) * slot_count]
+        mine_norms = square_norms(mine)
+        total = start_sums[repeat, :, :paths]
+        if repeat > 0:
+            total = total + a_weight[repeat] * start_sums[repeat, :, paths:]
+        for earlier in range(repeat):
+            cross = kernel_apply(
+                mine, mine_norms, step_rows[earlier], step_norms[earlier], updates[earlier]
+            )
+            total = total + b_weight[repeat][earlier] * cross
+        product = total / root_count
         gradient = jnp.where(
             is_live[:, None], product + NOISE * coefficients[local_rows] - targets[local_rows], 0.0
         )
-        velocity = (MOMENTUM * velocity).at[local_rows].add(-RATE * gradient)
+        step_update = -RATE * gradient
+        velocity = (MOMENTUM * velocity).at[local_rows].add(step_update)
         coefficients = coefficients + velocity
+        if repeat < steps - 1:
+            updates.append(gather_blocks(step_update, "blk").reshape(n_blk * slot_count, paths))
+
     own_sum = kernel_apply(candidates, square_norms(candidates), records, work_norms, coefficients)
     next_sum = kernel_apply(neighbour, square_norms(neighbour), records, work_norms, coefficients)
-    own_sum, next_sum = (own_sum, next_sum)
     first_part = prior_values(candidates, frequencies, phases, prior_weight) + own_sum / root_count
     next_term = next_sum / root_count
-    passed = passed_along(first_part, "blk", 1)
-    scores = passed_along(passed + next_term, "blk", 1)
+    scores = passed_along(first_part, "blk", 2) + passed_along(next_term, "blk", 1)
     squares_local = jnp.sum(scores * scores, axis=1)
     summed = lax.psum(squares_local, "path")
     path_rms = jnp.sqrt(summed / (scores.shape[1] * lax.axis_size("path")) + EPSILON)

time: 2490 us -> 266 us (0.11)
  waiting for transfers between devices: 2340 us -> 103 us
    psum x3 -> x0, waiting for transfers between devices: 2130 us -> none  [shards(): lax.psum(kernel_apply(gathered, gathered_norms, records, work_norms, work...]
    all_gather x3 -> x1, waiting for transfers between devices: 202 us -> 69.7 us  [shards(): gathered = lax.all_gather(own_rows, 'blk', axis=0, tiled=False)]
    all_to_all x0 -> x3, waiting for transfers between devices: none -> 28.1 us  [the longest x2 19.1 us: gather_blocks(): got = lax.all_to_all(spread, axis, 0, 0, tiled=True)]
  transfers between devices with their start and end apart: 9 -> 7, of which waited for: 8 -> 5; matrix products, arithmetic and copies ran while one was open for 3% -> 17% of each run, Pallas kernels for 0% -> 0%
where the time goes in v1:
time: 266 us; the launch traced here: 261 us
  waiting for transfers between devices  103 us (39%)
  matrix products  59.8 us (22%)
  local copies, waits for them, and re-layouts  27.6 us (10%)
  starting transfers between devices  24.5 us (9%)
  other arithmetic  24 us (9%)
  between operations  14.5 us (5%)
  blocking collectives  8.09 us (3%)
    all_gather x1, waiting for transfers between devices, shards(): gathered = lax.all_gather(own_rows, 'blk', axis=0, tiled=False)  69.7 us
    dot_general x6, matrix products, kernel_apply(): return jnp.dot(kernel_tile, weights, precision=lax.Precision.HIGHEST)  31.5 us
    all_to_all x2, waiting for transfers between devices, gather_blocks(): got = lax.all_to_all(spread, axis, 0, 0, tiled=True)  19.1 us
    dot_general x6, matrix products, kernel_apply(): lax.dot_general(left_rows, right_rows, (((1,), (1,)), ((), ())), preferre...  16.8 us
    all_to_all x2, starting transfers between devices, gather_blocks(): got = lax.all_to_all(spread, axis, 0, 0, tiled=True)  14.4 us
    reduce_sum x6, other arithmetic, square_norms(): return jnp.sum(widened * widened, axis=1)  10.8 us
    dot_general x1, matrix products, prior_values(): return jnp.dot(features, prior_weight, precision=lax.Precision.HIGHEST)  9.4 us
    all_to_all x1, waiting for transfers between devices, sum_to_owners(): got = lax.all_to_all(flat, axis, 0, 0, tiled=True)  8.97 us
  transfers between devices with their start and end apart: 7, of which 5 were waited for; matrix products, arithmetic and copies ran while one was open for 17% of the time, Pallas kernels for 0%

profile of v1, /device:TPU:1, one launch (start us, length us, event | category | flops | bytes accessed | tf_op | source)
XLA Modules:
  0.0 261.0 jit_solution(8226198046919181494)
XLA Ops:
  8.2 2.7 %gather_fusion = bf16[72,512]{1,0:T(8,128)(2,1)} fusion(bf16[1024,512]{1,0:T(8,128)(2,1)} %param.10, s32[1024]{0:T(1024)S(1)} %pad_clamp_fusion.3), kind=kCustom, calls=%fused_computation | custom fusion | bytes 147744 | tf_op jit(solution)/shard_map/gather | solution.py:88
  10.9 2.8 %collective-permute-start.1 = (bf16[512,512]{1,0:T(8,128)(2,1)}, bf16[512,512]{1,0:T(8,128)(2,1)}, u32[]{:S(2)}, u32[]{:S(2)}) collective-permute-start(bf16[512,512]{1,0:T(8,128)(2,1)} %param.16), channel_id=1, source_target_pairs={{0,4},{4,8},{8,12},{12,16},{16,20},{20,24},{24,28},{28,32},{32,36}... | collective-permute-start | bytes 1572872 | tf_op jit(solution)/shard_map/ppermute | solution.py:17
  21.8 3.2 %fusion.112 = f32[512,1024]{1,0:T(8,128)} fusion(bf16[512,512]{1,0:T(8,128)(2,1)} %param.16, bf16[1024,512]{1,0:T(8,128)(2,1)S(1)} %copy-done.1), kind=kOutput, calls=%fused_computation.153 | convolution fusion | flops 536870912 | bytes 3670016 | tf_op jit(solution)/shard_map/dot_general | solution.py:26
  38.2 3.2 %fusion.113 = f32[512,1024]{1,0:T(8,128)} fusion(bf16[512,512]{1,0:T(8,128)(2,1)} %collective-permute-done.1, bf16[1024,512]{1,0:T(8,128)(2,1)S(1)} %copy-done.1), kind=kOutput, calls=%fused_computation.154 | convolution fusion | flops 536870912 | bytes 3670016 | tf_op jit(solution)/shard_map/dot_general | solution.py:26
  41.3 69.7 %all-gather.3.cloned.1.call-done = bf16[4608,512]{1,0:T(8,128)(2,1)} async-done(((bf16[72,512]{1,0:T(8,128)(2,1)}), bf16[4608,512]{1,0:T(8,128)(2,1)}) %all-gather.3.cloned.1.call-update) | async-done | bytes 4718608 | tf_op jit(solution)/shard_map/all_gather | solution.py:89
  111.1 3.5 %multiply_reduce_fusion = f32[64,72]{1,0:T(8,128)S(1)} fusion(bf16[64,72,512]{2,1,0:T(8,128)(2,1)} %bitcast.52), kind=kLoop, calls=%fused_computation.23 | loop fusion | flops 7073280 | bytes 4737024 | tf_op jit(solution)/shard_map/reduce_sum | solution.py:22
  114.7 7.5 %fusion.110 = f32[4608,1024]{1,0:T(8,128)S(1)} fusion(bf16[4608,512]{1,0:T(8,128)(2,1)} %all-gather.3.cloned.1.call-done, bf16[1024,512]{1,0:T(8,128)(2,1)S(1)} %copy-done.1), kind=kOutput, calls=%fused_computation.151 | convolution fusion | flops 4831838208 | bytes 24641536 | tf_op jit(solution)/shard_map/dot_general | solution.py:26
  122.2 19.1 %fusion = f32[4608,32]{1,0:T(8,128)} fusion(f32[4608,1024]{1,0:T(8,128)S(1)} %fusion.110, f32[1024]{0:T(1024)S(1)} %multiply_reduce_fusion.3, f32[4608]{0:T(1024)S(1)} %add.210, f32[1024,16]{0,1:T(8,128)S(1)} %copy-done.13, f32[1024,16]{0,1:T(8,128)S(1)} %copy-done.11), kind=kOutput, calls=%fused_computation.10 | convolution fusion | flops 1840283648 | bytes 19617792 | tf_op jit(solution)/shard_map/dot_general | solution.py:31
  141.2 3.3 %all_to_all.18 = f32[64,1,2304]{2,1,0:T(1,128)} reshape(f32[4608,32]{1,0:T(8,128)} %fusion) | data formatting | bytes 1179648 | tf_op jit(solution)/shard_map/all_to_all | solution.py:54
  144.5 5.1 %all-to-all-start = ((f32[64,1,2304]{2,1,0:T(1,128)}), f32[64,1,2304]{2,1,0:T(1,128)S(1)}, u32[]{:S(2)}, u32[]{:S(2)}) async-start(f32[64,1,2304]{2,1,0:T(1,128)} %all_to_all.18), calls=%async_computation | async-start | bytes 1179648 | tf_op jit(solution)/shard_map/all_to_all | solution.py:54
  149.6 2.6 multiply_reduce_fusion.1
  157.4 9.0 %all-to-all-done = f32[64,1,2304]{2,1,0:T(1,128)S(1)} async-done(((f32[64,1,2304]{2,1,0:T(1,128)}), f32[64,1,2304]{2,1,0:T(1,128)S(1)}, u32[]{:S(2)}, u32[]{:S(2)}) %all-to-all-start) | async-done | bytes 589856 | tf_op jit(solution)/shard_map/all_to_all | solution.py:54
  168.1 10.0 %all-to-all-start.1 = ((f32[64,1,384]{2,1,0:T(1,128)}), f32[64,1,384]{2,1,0:T(1,128)S(1)}, u32[]{:S(2)}, u32[]{:S(2)}) async-start(f32[64,1,384]{2,1,0:T(1,128)} %broadcast_in_dim.39), calls=%async_computation.1 | async-start | bytes 196608 | tf_op jit(solution)/shard_map/all_to_all | solution.py:47
  182.0 9.1 %all-to-all-done.1 = f32[64,1,384]{2,1,0:T(1,128)S(1)} async-done(((f32[64,1,384]{2,1,0:T(1,128)}), f32[64,1,384]{2,1,0:T(1,128)S(1)}, u32[]{:S(2)}, u32[]{:S(2)}) %all-to-all-start.1) | async-done | bytes 98336 | tf_op jit(solution)/shard_map/all_to_all | solution.py:47
  191.7 2.3 fusion.68
  194.8 2.5 scatter_fusion.1
  200.5 4.4 %all-to-all-start.2 = ((f32[64,1,384]{2,1,0:T(1,128)}), f32[64,1,384]{2,1,0:T(1,128)S(1)}, u32[]{:S(2)}, u32[]{:S(2)}) async-start(f32[64,1,384]{2,1,0:T(1,128)} %broadcast_in_dim.74), calls=%async_computation.2 | async-start | bytes 196608 | tf_op jit(solution)/shard_map/all_to_all | solution.py:47
  205.0 2.3 fusion.63
  207.3 10.0 %all-to-all-done.2 = f32[64,1,384]{2,1,0:T(1,128)S(1)} async-done(((f32[64,1,384]{2,1,0:T(1,128)}), f32[64,1,384]{2,1,0:T(1,128)S(1)}, u32[]{:S(2)}, u32[]{:S(2)}) %all-to-all-start.2) | async-done | bytes 98336 | tf_op jit(solution)/shard_map/all_to_all | solution.py:47
  220.3 4.1 %fusion.52 = f32[512,16]{0,1:T(8,128)S(1)} fusion(f32[1024,16]{1,0:T(8,128)S(1)} %add.238, f32[512,1024]{1,0:T(8,128)} %fusion.112, f32[1024]{0:T(1024)S(1)} %copy-done.22, f32[512]{0:T(512)S(1)} %copy-done.23), kind=kOutput, calls=%fused_computation.67 | convolution fusion | flops 103817216 | bytes 2201600 | tf_op jit(solution)/shard_map/dot_general | solution.py:31
  224.5 9.4 %fusion.49 = f32[512,16]{0,1:T(8,128)S(1)} fusion(f32[512,16]{0,1:T(8,128)S(1)} %fusion.52, f32[1024,16]{0,1:T(8,128)S(1)} %copy-done.12, f32[512,1024]{1,0:T(8,128)S(1)} %copy-done.2, f32[1024]{0:T(1024)S(1)} %copy-done.20), kind=kOutput, calls=%fused_computation.66 | convolution fusion | flops 102244352 | bytes 2232320 | tf_op jit(solution)/shard_map/dot_general | solution.py:40
  234.3 2.4 fusion.55
  240.0 4.8 %collective-permute-done = f32[512,16]{0,1:T(8,128)S(1)} collective-permute-done((f32[512,16]{0,1:T(8,128)S(1)}, f32[512,16]{0,1:T(8,128)S(1)}, u32[]{:S(2)}, u32[]{:S(2)}) %collective-permute-start) | collective-permute-done | bytes 32800 | tf_op jit(solution)/shard_map/ppermute | solution.py:17
  245.5 8.1 %psum.7 = f32[512]{0:T(512)S(1)} all-reduce(f32[512]{0:T(512)S(1)} %get-tuple-element.20), channel_id=1, replica_groups=mesh['blk'=64,'path'=4] {'path'}, use_global_device_ids=true, to_apply=%region_13.14 | all-reduce | flops 512 | bytes 4096 | tf_op jit(solution)/shard_map/psum | solution.py:134
  (136 shorter events, 45.6 us)
Async XLA Ops:
  7.2 27.2 %copy-start = (bf16[512,1024]{1,0:T(8,128)(2,1)S(1)}, bf16[512,1024]{1,0:T(8,128)(2,1)}, u32[]{:S(2)}) copy-start(bf16[512,1024]{1,0:T(8,128)(2,1)} %param.17) | copy-start | bytes 3145732
  7.2 14.7 %copy-start.1 = (bf16[1024,512]{1,0:T(8,128)(2,1)S(1)}, bf16[1024,512]{1,0:T(8,128)(2,1)}, u32[]{:S(2)}) copy-start(bf16[1024,512]{1,0:T(8,128)(2,1)} %param.10) | copy-start | bytes 3145732
  7.2 103.9 %all-gather.3.cloned.1.call-start = ((), (), s32[]{:S(2)}) async-start(), calls=%async_computation.3 | async-start | bytes 4792320 | tf_op jit(solution)/shard_map/all_gather | solution.py:89
  10.9 25.5 %collective-permute-start.1 = (bf16[512,512]{1,0:T(8,128)(2,1)}, bf16[512,512]{1,0:T(8,128)(2,1)}, u32[]{:S(2)}, u32[]{:S(2)}) collective-permute-start(bf16[512,512]{1,0:T(8,128)(2,1)} %param.16), channel_id=1, source_target_pairs={{0,4},{4,8},{8,12},{12,16},{16,20},{20,24},{24,28},{28,32},{32,36}... | collective-permute-start | bytes 1572872 | tf_op jit(solution)/shard_map/ppermute | solution.py:17
  18.3 13.5 %copy-start.15 = (s32[1024]{0:T(1024)}, s32[1024]{0:T(1024)S(1)}, u32[]{:S(2)}) copy-start(s32[1024]{0:T(1024)S(1)} %get-tuple-element.41) | copy-start | bytes 12292
  19.1 7.2 %copy-start.10 = (f32[1024,16]{0,1:T(8,128)S(1)}, f32[1024,16]{0,1:T(8,128)}, u32[]{:S(2)}) copy-start(f32[1024,16]{0,1:T(8,128)} %param.13) | copy-start | bytes 196612
  25.1 9.3 %copy-start.3 = (bf16[512,512]{1,0:T(8,128)(2,1)S(1)}, bf16[512,512]{1,0:T(8,128)(2,1)}, u32[]{:S(2)}) copy-start(bf16[512,512]{1,0:T(8,128)(2,1)} %param.16) | copy-start | bytes 1572868
  34.4 87.8 %copy-start.21 = (f32[1024]{0:T(1024)}, f32[1024]{0:T(1024)S(1)}, u32[]{:S(2)}) copy-start(f32[1024]{0:T(1024)S(1)} %multiply_reduce_fusion.3) | copy-start | bytes 12292
  114.7 7.5 %copy-start.13 = (f32[1024,16]{0,1:T(8,128)S(1)}, f32[1024,16]{0,1:T(8,128)}, u32[]{:S(2)}) copy-start(f32[1024,16]{0,1:T(8,128)} %param.12) | copy-start | bytes 196612
  144.5 21.9 %all-to-all-start = ((f32[64,1,2304]{2,1,0:T(1,128)}), f32[64,1,2304]{2,1,0:T(1,128)S(1)}, u32[]{:S(2)}, u32[]{:S(2)}) async-start(f32[64,1,2304]{2,1,0:T(1,128)} %all_to_all.18), calls=%async_computation | async-start | bytes 1179648 | tf_op jit(solution)/shard_map/all_to_all | solution.py:54
  155.7 22.4 %copy-start.4 = (f32[1024,16]{1,0:T(8,128)S(1)}, f32[1024,16]{1,0:T(8,128)}, u32[]{:S(2)}) copy-start(f32[1024,16]{1,0:T(8,128)} %copy.65) | copy-start | bytes 196612
  168.1 23.1 %all-to-all-start.1 = ((f32[64,1,384]{2,1,0:T(1,128)}), f32[64,1,384]{2,1,0:T(1,128)S(1)}, u32[]{:S(2)}, u32[]{:S(2)}) async-start(f32[64,1,384]{2,1,0:T(1,128)} %broadcast_in_dim.39), calls=%async_computation.1 | async-start | bytes 196608 | tf_op jit(solution)/shard_map/all_to_all | solution.py:47
  179.9 11.3 %copy-start.5 = (f32[1024,16]{1,0:T(8,128)}, f32[1024,16]{1,0:T(8,128)S(1)}, u32[]{:S(2)}) copy-start(f32[1024,16]{1,0:T(8,128)S(1)} %get-tuple-element.27) | copy-start | bytes 196612
  179.9 14.9 %copy-start.19 = (s32[24]{0:T(128)S(1)}, s32[24]{0:T(128)}, u32[]{:S(2)}) copy-start(s32[24]{0:T(128)} %copy-done.18) | copy-start | bytes 292
  198.4 19.4 %copy-start.14 = (f32[24,16]{0,1:T(8,128)S(1)}, f32[24,16]{0,1:T(8,128)}, u32[]{:S(2)}) copy-start(f32[24,16]{0,1:T(8,128)} %copy.82) | copy-start | bytes 4612
  198.4 19.4 %copy-start.25 = (pred[24]{0:T(512)(128)(4,1)S(1)}, pred[24]{0:T(512)(128)(4,1)}, u32[]{:S(2)}) copy-start(pred[24]{0:T(512)(128)(4,1)} %iota_compare_fusion) | copy-start | bytes 76
  198.4 20.8 %copy-start.17 = (s32[24]{0:T(128)S(1)}, s32[24]{0:T(128)}, u32[]{:S(2)}) copy-start(s32[24]{0:T(128)} %copy-done.16) | copy-start | bytes 292
  200.5 16.7 %all-to-all-start.2 = ((f32[64,1,384]{2,1,0:T(1,128)}), f32[64,1,384]{2,1,0:T(1,128)S(1)}, u32[]{:S(2)}, u32[]{:S(2)}) async-start(f32[64,1,384]{2,1,0:T(1,128)} %broadcast_in_dim.74), calls=%async_computation.2 | async-start | bytes 196608 | tf_op jit(solution)/shard_map/all_to_all | solution.py:47
  207.3 13.0 %copy-start.22 = (f32[1024]{0:T(1024)S(1)}, f32[1024]{0:T(1024)}, u32[]{:S(2)}) copy-start(f32[1024]{0:T(1024)} %copy-done.21) | copy-start | bytes 12292
  207.3 13.0 %copy-start.23 = (f32[512]{0:T(512)S(1)}, f32[512]{0:T(512)}, u32[]{:S(2)}) copy-start(f32[512]{0:T(512)} %multiply_reduce_fusion.5) | copy-start | bytes 6148
  220.3 14.0 %copy-start.7 = (f32[512,1024]{1,0:T(8,128)S(1)}, f32[512,1024]{1,0:T(8,128)}, u32[]{:S(2)}) copy-start(f32[512,1024]{1,0:T(8,128)} %fusion.113) | copy-start | bytes 6291460
  220.3 14.0 %copy-start.24 = (f32[512]{0:T(512)S(1)}, f32[512]{0:T(512)}, u32[]{:S(2)}) copy-start(f32[512]{0:T(512)} %multiply_reduce_fusion.4) | copy-start | bytes 6148
  233.9 11.0 %collective-permute-start = (f32[512,16]{0,1:T(8,128)S(1)}, f32[512,16]{0,1:T(8,128)S(1)}, u32[]{:S(2)}, u32[]{:S(2)}) collective-permute-start(f32[512,16]{0,1:T(8,128)S(1)} %fusion.49), channel_id=1, source_target_pairs={{0,8},{4,12},{8,16},{12,20},{16,24},{20,28},{24,32},{28,36},{32,40... | collective-permute-start | bytes 98312 | tf_op jit(solution)/shard_map/ppermute | solution.py:17
  236.7 8.2 %collective-permute-start.2 = (f32[512,16]{0,1:T(8,128)S(1)}, f32[512,16]{0,1:T(8,128)S(1)}, u32[]{:S(2)}, u32[]{:S(2)}) collective-permute-start(f32[512,16]{0,1:T(8,128)S(1)} %fusion.55), channel_id=1, source_target_pairs={{0,4},{4,8},{8,12},{12,16},{16,20},{20,24},{24,28},{28,32},{32,36}... | collective-permute-start | bytes 98312 | tf_op jit(solution)/shard_map/ppermute | solution.py:17
  (9 other events, 40.9 us)
Sparse Core Ops, SparseCore 0:
  11.5 99.4 all-gather.2

commit v2 on v1

--- a/solution.py
+++ b/solution.py
@@ -22,13 +22,17 @@
     return jnp.sum(widened * widened, axis=1)
 
 
-def kernel_apply(left_rows, left_norms, right_rows, right_norms, weights):
+def kernel_tile_of(left_rows, left_norms, right_rows, right_norms):
     dot_values = lax.dot_general(
         left_rows, right_rows, (((1,), (1,)), ((), ())), preferred_element_type=jnp.float32
     )
     distance = left_norms[:, None] + right_norms[None, :] - 2.0 * dot_values
-    kernel_tile = SIGNAL * jnp.exp(-distance / left_rows.shape[1])
-    return jnp.dot(kernel_tile, weights, precision=lax.Precision.HIGHEST)
+    return SIGNAL * jnp.exp(-distance / left_rows.shape[1])
+
+
+def kernel_apply(left_rows, left_norms, right_rows, right_norms, weights):
+    kernel_tile = kernel_tile_of(left_rows, left_norms, right_rows, right_norms)
+    return jnp.dot(kernel_tile, weights, precision=lax.Precision.HIGH)
 
 
 def prior_values(cand_rows, frequencies, phases, prior_weight):
@@ -99,7 +103,15 @@
     start_sums = sum_to_owners(partial.reshape(n_blk, steps * slot_count, 2 * paths), "blk")
     start_sums = start_sums.reshape(steps, slot_count, 2 * paths)
 
-    a_weight, b_weight = velocity_weights(steps)
+    a_weight, b_weight = velocity_weights(steps + 1)
+    own_rows_norms = square_norms(own_rows)
+    cand_norms = square_norms(candidates)
+    neighbour_norms = square_norms(neighbour)
+    own_start = kernel_apply(candidates, cand_norms, records, work_norms, start_weights)
+    next_start = kernel_apply(neighbour, neighbour_norms, records, work_norms, start_weights)
+    own_slots = kernel_tile_of(candidates, cand_norms, own_rows, own_rows_norms)
+    next_slots = kernel_tile_of(neighbour, neighbour_norms, own_rows, own_rows_norms)
+    weighted_updates = []
     updates = []
     for repeat in range(steps):
         local_rows = block_local[repeat]
@@ -122,11 +134,21 @@
         step_update = -RATE * gradient
         velocity = (MOMENTUM * velocity).at[local_rows].add(step_update)
         coefficients = coefficients + velocity
+        weighted_updates.append(b_weight[steps][repeat] * step_update)
         if repeat < steps - 1:
             updates.append(gather_blocks(step_update, "blk").reshape(n_blk * slot_count, paths))
 
-    own_sum = kernel_apply(candidates, square_norms(candidates), records, work_norms, coefficients)
-    next_sum = kernel_apply(neighbour, square_norms(neighbour), records, work_norms, coefficients)
+    slot_weights = jnp.concatenate(weighted_updates, axis=0)
+    own_sum = (
+        own_start[:, :paths]
+        + a_weight[steps] * own_start[:, paths:]
+        + jnp.dot(own_slots, slot_weights, precision=lax.Precision.HIGH)
+    )
+    next_sum = (
+        next_start[:, :paths]
+        + a_weight[steps] * next_start[:, paths:]
+        + jnp.dot(next_slots, slot_weights, precision=lax.Precision.HIGH)
+    )
     first_part = prior_values(candidates, frequencies, phases, prior_weight) + own_sum / root_count
     next_term = next_sum / root_count
     scores = passed_along(first_part, "blk", 2) + passed_along(next_term, "blk", 1)

time: 266 us -> 256 us (0.962); the launches traced: 261 us -> 254 us
  matrix products: 59.8 us -> 48.4 us
  local copies, waits for them, and re-layouts: 27.6 us -> 32.9 us
    dot_general x12 -> x16, matrix products: 48.3 us -> 37.1 us  [the longest x6 21.1 us: kernel_apply(): return jnp.dot(kernel_tile, weights, precision=lax.Precision.HIGH)]
    reduce_sum x6 -> x7, other arithmetic: 10.8 us -> 6.95 us  [square_norms(): return jnp.sum(widened * widened, axis=1)]
    unnamed x61 -> x70, local copies, waits for them, and re-layouts: 3.83 us -> 7.29 us
    gather x6, local copies, waits for them, and re-layouts: 2.04 us -> 4.98 us  [shards(): coefficients[local_rows]]
  transfers between devices with their start and end apart: 7 -> 7, of which waited for: 5 -> 5; matrix products, arithmetic and copies ran while one was open for 17% -> 22% of each run, Pallas kernels for 0% -> 0%
where the time goes in v2:
time: 256 us; the launch traced here: 254 us
  waiting for transfers between devices  103 us (40%)
  matrix products  48.4 us (19%)
  local copies, waits for them, and re-layouts  32.9 us (13%)
  starting transfers between devices  24.4 us (10%)
  other arithmetic  22.6 us (9%)
  between operations  14.5 us (6%)
  blocking collectives  8.8 us (3%)
    all_gather x1, waiting for transfers between devices, shards(): gathered = lax.all_gather(own_rows, 'blk', axis=0, tiled=False)  69 us
    all_to_all x2, waiting for transfers between devices, gather_blocks(): got = lax.all_to_all(spread, axis, 0, 0, tiled=True)  21.2 us
    dot_general x6, matrix products, kernel_apply(): return jnp.dot(kernel_tile, weights, precision=lax.Precision.HIGH)  21.1 us
    all_to_all x2, starting transfers between devices, gather_blocks(): got = lax.all_to_all(spread, axis, 0, 0, tiled=True)  15.2 us
    dot_general x8, matrix products, kernel_tile_of(): lax.dot_general(left_rows, right_rows, (((1,), (1,)), ((), ())), preferre...  13.8 us
    dot_general x1, matrix products, prior_values(): return jnp.dot(features, prior_weight, precision=lax.Precision.HIGHEST)  9.14 us
    all_to_all x1, waiting for transfers between devices, sum_to_owners(): got = lax.all_to_all(flat, axis, 0, 0, tiled=True)  9.05 us
    psum x1, blocking collectives, shards(): summed = lax.psum(squares_local, 'path')  8.8 us
  transfers between devices with their start and end apart: 7, of which 5 were waited for; matrix products, arithmetic and copies ran while one was open for 22% of the time, Pallas kernels for 0%

profile of v2, /device:TPU:1, one launch (start us, length us, event | category | flops | bytes accessed | tf_op | source)
XLA Modules:
  0.0 254.3 jit_solution(2650041016654992201)
XLA Ops:
  8.2 2.7 %gather_fusion = bf16[72,512]{1,0:T(8,128)(2,1)} fusion(bf16[1024,512]{1,0:T(8,128)(2,1)} %param.10, s32[1024]{0:T(1024)S(1)} %pad_clamp_fusion.3), kind=kCustom, calls=%fused_computation | custom fusion | bytes 147744 | tf_op jit(solution)/shard_map/gather | solution.py:92
  11.0 2.8 %collective-permute-start.1 = (bf16[512,512]{1,0:T(8,128)(2,1)}, bf16[512,512]{1,0:T(8,128)(2,1)S(1)}, u32[]{:S(2)}, u32[]{:S(2)}) collective-permute-start(bf16[512,512]{1,0:T(8,128)(2,1)} %param.16), channel_id=1, source_target_pairs={{0,4},{4,8},{8,12},{12,16},{16,20},{20,24},{24,28},{28,32},{32,36}... | collective-permute-start | bytes 1572872 | tf_op jit(solution)/shard_map/ppermute | solution.py:17
  33.1 2.1 fusion.36
  36.1 2.1 fusion.123
  40.1 2.1 fusion.28
  42.2 69.0 %all-gather.3.cloned.1.call-done = bf16[4608,512]{1,0:T(8,128)(2,1)} async-done(((bf16[72,512]{1,0:T(8,128)(2,1)}), bf16[4608,512]{1,0:T(8,128)(2,1)}) %all-gather.3.cloned.1.call-update) | async-done | bytes 4718608 | tf_op jit(solution)/shard_map/all_gather | solution.py:93
  111.1 3.5 %multiply_reduce_fusion = f32[64,72]{1,0:T(8,128)S(1)} fusion(bf16[64,72,512]{2,1,0:T(8,128)(2,1)} %bitcast.71), kind=kLoop, calls=%fused_computation.23 | loop fusion | flops 7073280 | bytes 4737024 | tf_op jit(solution)/shard_map/reduce_sum | solution.py:22
  114.7 7.5 %fusion.122 = f32[4608,1024]{1,0:T(8,128)S(1)} fusion(bf16[4608,512]{1,0:T(8,128)(2,1)} %all-gather.3.cloned.1.call-done, bf16[1024,512]{1,0:T(8,128)(2,1)S(1)} %copy-done.1), kind=kOutput, calls=%fused_computation.180 | convolution fusion | flops 4831838208 | bytes 24641536 | tf_op jit(solution)/shard_map/dot_general | solution.py:26
  122.3 11.1 %fusion = f32[4608,32]{1,0:T(8,128)S(1)} fusion(f32[1024,32]{0,1:T(8,128)S(1)} %copy-done.13, f32[4608,1024]{1,0:T(8,128)S(1)} %fusion.122, f32[1024]{0:T(1024)S(1)} %multiply_reduce_fusion.3, f32[4608]{0:T(1024)S(1)} %add.246), kind=kOutput, calls=%fused_computation.10 | convolution fusion | flops 934281216 | bytes 19617792 | tf_op jit(solution)/shard_map/dot_general | solution.py:35
  133.4 2.1 all_to_all.18
  135.4 5.1 %all-to-all-start = ((f32[64,1,2304]{2,1,0:T(1,128)}), f32[64,1,2304]{2,1,0:T(1,128)S(1)}, u32[]{:S(2)}, u32[]{:S(2)}) async-start(f32[64,1,2304]{2,1,0:T(1,128)} %all_to_all.18), calls=%async_computation | async-start | bytes 1179648 | tf_op jit(solution)/shard_map/all_to_all | solution.py:58
  140.5 2.6 %multiply_reduce_fusion.1 = (f32[64,24]{1,0:T(8,128)S(1)}, f32[64,24]{1,0:T(8,128)S(1)}) fusion(bf16[64,72,512]{2,1,0:T(8,128)(2,1)} %bitcast.72), kind=kLoop, calls=%fused_computation.24 | loop fusion | flops 4715520 | bytes 3158016 | tf_op jit(solution)/shard_map/reduce_sum | solution.py:22
  143.3 2.1 fusion.119
  148.3 9.0 %all-to-all-done = f32[64,1,2304]{2,1,0:T(1,128)S(1)} async-done(((f32[64,1,2304]{2,1,0:T(1,128)}), f32[64,1,2304]{2,1,0:T(1,128)S(1)}, u32[]{:S(2)}, u32[]{:S(2)}) %all-to-all-start) | async-done | bytes 589856 | tf_op jit(solution)/shard_map/all_to_all | solution.py:58
  159.6 10.2 %all-to-all-start.1 = ((f32[64,1,384]{2,1,0:T(1,128)}), f32[64,1,384]{2,1,0:T(1,128)}, u32[]{:S(2)}, u32[]{:S(2)}) async-start(f32[64,1,384]{2,1,0:T(1,128)} %broadcast_in_dim.39), calls=%async_computation.1 | async-start | bytes 196608 | tf_op jit(solution)/shard_map/all_to_all | solution.py:51
  171.9 10.7 %all-to-all-done.1 = f32[64,1,384]{2,1,0:T(1,128)} async-done(((f32[64,1,384]{2,1,0:T(1,128)}), f32[64,1,384]{2,1,0:T(1,128)}, u32[]{:S(2)}, u32[]{:S(2)}) %all-to-all-start.1) | async-done | bytes 98336 | tf_op jit(solution)/shard_map/all_to_all | solution.py:51
  184.1 2.0 broadcast_multiply_fusion.3
  191.5 5.0 %all-to-all-start.2 = ((f32[64,1,384]{2,1,0:T(1,128)}), f32[64,1,384]{2,1,0:T(1,128)}, u32[]{:S(2)}, u32[]{:S(2)}) async-start(f32[64,1,384]{2,1,0:T(1,128)} %broadcast_in_dim.42), calls=%async_computation.2 | async-start | bytes 196608 | tf_op jit(solution)/shard_map/all_to_all | solution.py:51
  198.4 10.5 %all-to-all-done.2 = f32[64,1,384]{2,1,0:T(1,128)} async-done(((f32[64,1,384]{2,1,0:T(1,128)}), f32[64,1,384]{2,1,0:T(1,128)}, u32[]{:S(2)}, u32[]{:S(2)}) %all-to-all-start.2) | async-done | bytes 98336 | tf_op jit(solution)/shard_map/all_to_all | solution.py:51
  210.7 2.1 reshape_reshape.12
  217.4 9.1 %fusion.56 = f32[512,16]{0,1:T(8,128)S(1)} fusion(f32[512,16]{0,1:T(8,128)S(1)} %fusion.60, f32[1024,16]{0,1:T(8,128)S(1)} %copy-done.11, f32[512,1024]{1,0:T(8,128)S(1)} %copy-done.3, f32[1024]{0:T(1024)S(1)} %copy-done.23), kind=kOutput, calls=%fused_computation.75 | convolution fusion | flops 102244352 | bytes 2232320 | tf_op jit(solution)/shard_map/dot_general | solution.py:44
  227.6 2.5 scatter_fusion.2
  233.9 3.5 %collective-permute-done = f32[512,16]{0,1:T(8,128)S(1)} collective-permute-done((f32[512,16]{0,1:T(8,128)S(1)}, f32[512,16]{0,1:T(8,128)S(1)}, u32[]{:S(2)}, u32[]{:S(2)}) %collective-permute-start) | collective-permute-done | bytes 32800 | tf_op jit(solution)/shard_map/ppermute | solution.py:17
  238.1 8.8 %psum.7 = f32[512]{0:T(512)S(1)} all-reduce(f32[512]{0:T(512)S(1)} %get-tuple-element.20), channel_id=1, replica_groups=mesh['blk'=64,'path'=4] {'path'}, use_global_device_ids=true, to_apply=%region_14.15 | all-reduce | flops 512 | bytes 4096 | tf_op jit(solution)/shard_map/psum | solution.py:156
  (151 shorter events, 51.8 us)
Async XLA Ops:
  7.2 28.9 %copy-start = (bf16[512,1024]{1,0:T(8,128)(2,1)S(1)}, bf16[512,1024]{1,0:T(8,128)(2,1)}, u32[]{:S(2)}) copy-start(bf16[512,1024]{1,0:T(8,128)(2,1)} %param.17) | copy-start | bytes 3145732
  7.2 24.8 %copy-start.1 = (bf16[1024,512]{1,0:T(8,128)(2,1)S(1)}, bf16[1024,512]{1,0:T(8,128)(2,1)}, u32[]{:S(2)}) copy-start(bf16[1024,512]{1,0:T(8,128)(2,1)} %param.10) | copy-start | bytes 3145732
  7.2 24.6 %copy-start.2 = (bf16[512,512]{1,0:T(8,128)(2,1)S(1)}, bf16[512,512]{1,0:T(8,128)(2,1)}, u32[]{:S(2)}) copy-start(bf16[512,512]{1,0:T(8,128)(2,1)} %param.16) | copy-start | bytes 1572868
  7.2 16.9 %copy-start.9 = (f32[1024,16]{0,1:T(8,128)S(1)}, f32[1024,16]{0,1:T(8,128)}, u32[]{:S(2)}) copy-start(f32[1024,16]{0,1:T(8,128)} %param.11) | copy-start | bytes 196612
  7.2 16.9 %copy-start.10 = (f32[1024,16]{0,1:T(8,128)S(1)}, f32[1024,16]{0,1:T(8,128)}, u32[]{:S(2)}) copy-start(f32[1024,16]{0,1:T(8,128)} %param.12) | copy-start | bytes 196612
  7.2 103.9 %all-gather.3.cloned.1.call-start = ((), (), s32[]{:S(2)}) async-start(), calls=%async_computation.3 | async-start | bytes 4792320 | tf_op jit(solution)/shard_map/all_gather | solution.py:93
  10.9 20.6 %copy-start.5 = (bf16[72,512]{1,0:T(8,128)(2,1)S(1)}, bf16[72,512]{1,0:T(8,128)(2,1)}, u32[]{:S(2)}) copy-start(bf16[72,512]{1,0:T(8,128)(2,1)} %gather_fusion) | copy-start | bytes 221188
  11.0 27.2 %collective-permute-start.1 = (bf16[512,512]{1,0:T(8,128)(2,1)}, bf16[512,512]{1,0:T(8,128)(2,1)S(1)}, u32[]{:S(2)}, u32[]{:S(2)}) collective-permute-start(bf16[512,512]{1,0:T(8,128)(2,1)} %param.16), channel_id=1, source_target_pairs={{0,4},{4,8},{8,12},{12,16},{16,20},{20,24},{24,28},{28,32},{32,36}... | collective-permute-start | bytes 1572872 | tf_op jit(solution)/shard_map/ppermute | solution.py:17
  16.4 16.7 %copy-start.19 = (s32[24]{0:T(128)}, s32[24]{0:T(128)S(1)}, u32[]{:S(2)}) copy-start(s32[24]{0:T(128)S(1)} %get-tuple-element.45) | copy-start | bytes 292
  24.1 15.9 %copy-start.12 = (f32[1024,32]{0,1:T(8,128)}, f32[1024,32]{0,1:T(8,128)S(1)}, u32[]{:S(2)}) copy-start(f32[1024,32]{0,1:T(8,128)S(1)} %get-tuple-element.30) | copy-start | bytes 393220
  31.7 113.7 %copy-start.16 = (f32[24]{0:T(128)}, f32[24]{0:T(128)S(1)}, u32[]{:S(2)}) copy-start(f32[24]{0:T(128)S(1)} %get-tuple-element.18) | copy-start | bytes 292
  135.4 21.9 %all-to-all-start = ((f32[64,1,2304]{2,1,0:T(1,128)}), f32[64,1,2304]{2,1,0:T(1,128)S(1)}, u32[]{:S(2)}, u32[]{:S(2)}) async-start(f32[64,1,2304]{2,1,0:T(1,128)} %all_to_all.18), calls=%async_computation | async-start | bytes 1179648 | tf_op jit(solution)/shard_map/all_to_all | solution.py:58
  146.6 23.4 %copy-start.7 = (f32[1024,16]{1,0:T(8,128)S(1)}, f32[1024,16]{1,0:T(8,128)}, u32[]{:S(2)}) copy-start(f32[1024,16]{1,0:T(8,128)} %copy.65) | copy-start | bytes 196612
  146.6 23.4 %copy-start.22 = (s32[24]{0:T(128)S(1)}, s32[24]{0:T(128)}, u32[]{:S(2)}) copy-start(s32[24]{0:T(128)} %copy-done.21) | copy-start | bytes 292
  146.6 24.3 %copy-start.6 = (f32[1024,16]{1,0:T(8,128)S(1)}, f32[1024,16]{1,0:T(8,128)}, u32[]{:S(2)}) copy-start(f32[1024,16]{1,0:T(8,128)} %copy.67) | copy-start | bytes 196612
  159.6 23.0 %all-to-all-start.1 = ((f32[64,1,384]{2,1,0:T(1,128)}), f32[64,1,384]{2,1,0:T(1,128)}, u32[]{:S(2)}, u32[]{:S(2)}) async-start(f32[64,1,384]{2,1,0:T(1,128)} %broadcast_in_dim.39), calls=%async_computation.1 | async-start | bytes 196608 | tf_op jit(solution)/shard_map/all_to_all | solution.py:51
  188.2 28.1 %copy-start.8 = (f32[512,72]{0,1:T(8,128)S(1)}, f32[512,72]{0,1:T(8,128)}, u32[]{:S(2)}) copy-start(f32[512,72]{0,1:T(8,128)} %fusion.55) | copy-start | bytes 442372
  188.2 29.1 %copy-start.3 = (f32[512,1024]{1,0:T(8,128)S(1)}, f32[512,1024]{1,0:T(8,128)}, u32[]{:S(2)}) copy-start(f32[512,1024]{1,0:T(8,128)} %fusion.123) | copy-start | bytes 6291460
  188.2 29.1 %copy-start.11 = (f32[1024,16]{0,1:T(8,128)S(1)}, f32[1024,16]{0,1:T(8,128)}, u32[]{:S(2)}) copy-start(f32[1024,16]{0,1:T(8,128)} %param.19) | copy-start | bytes 196612
  188.2 29.1 %copy-start.23 = (f32[1024]{0:T(1024)S(1)}, f32[1024]{0:T(1024)}, u32[]{:S(2)}) copy-start(f32[1024]{0:T(1024)} %param.18) | copy-start | bytes 12292
  191.5 17.5 %all-to-all-start.2 = ((f32[64,1,384]{2,1,0:T(1,128)}), f32[64,1,384]{2,1,0:T(1,128)}, u32[]{:S(2)}, u32[]{:S(2)}) async-start(f32[64,1,384]{2,1,0:T(1,128)} %broadcast_in_dim.42), calls=%async_computation.2 | async-start | bytes 196608 | tf_op jit(solution)/shard_map/all_to_all | solution.py:51
  210.7 16.9 %copy-start.18 = (s32[24]{0:T(128)S(1)}, s32[24]{0:T(128)}, u32[]{:S(2)}) copy-start(s32[24]{0:T(128)} %copy-done.17) | copy-start | bytes 292
  215.9 18.0 %collective-permute-start.2 = (f32[512,16]{0,1:T(8,128)S(1)}, f32[512,16]{0,1:T(8,128)S(1)}, u32[]{:S(2)}, u32[]{:S(2)}) collective-permute-start(f32[512,16]{0,1:T(8,128)S(1)} %fusion.59), channel_id=1, source_target_pairs={{0,4},{4,8},{8,12},{12,16},{16,20},{20,24},{24,28},{28,32},{32,36}... | collective-permute-start | bytes 98312 | tf_op jit(solution)/shard_map/ppermute | solution.py:17
  226.5 11.0 %collective-permute-start = (f32[512,16]{0,1:T(8,128)S(1)}, f32[512,16]{0,1:T(8,128)S(1)}, u32[]{:S(2)}, u32[]{:S(2)}) collective-permute-start(f32[512,16]{0,1:T(8,128)S(1)} %fusion.56), channel_id=1, source_target_pairs={{0,8},{4,12},{8,16},{12,20},{16,24},{20,28},{24,32},{28,36},{32,40... | collective-permute-start | bytes 98312 | tf_op jit(solution)/shard_map/ppermute | solution.py:17
  (13 other events, 98.4 us)
Sparse Core Ops, SparseCore 0:
  11.6 99.5 all-gather.2
